TPU v7x, 32 devices: a whole 2x2x4 slice. The times are simulated.
32 devices in a mesh: groups: 2 (over x), seq: 8 (over z, y), chan: 2 (over core).
Axes of the slice: x: 2, y: 2, z: 4, core: 2. Of those that a mesh axis runs over, the one named last changes fastest.
Arguments:
- cached_input: bfloat16 [2048, 4096], P(('groups', 'seq'), 'chan'), parts along dimension 0, may hold values from -6 to 6
- cached_gate: bfloat16 [2048, 4096], P(('groups', 'seq'), 'chan'), parts along dimension 0, may hold values from -6 to 6
- out_grad: bfloat16 [2048, 4096], P(('groups', 'seq'), 'chan'), parts along dimension 0, may hold values from -1.75 to 1.75
- filter_taps: bfloat16 [1024, 32], P('seq', 'chan'), may hold values from -6 to 6
- skip_gain: float32 [4096], P('chan'), may hold values from -1 to 1
Outputs:
- input_grad: bfloat16 [2048, 4096], P(('groups', 'seq'), 'chan'), parts along dimension 0
- filter_grad: float32 [2048, 32], P(('groups', 'seq'), 'chan'), parts along dimension 0
There are 2 independent parts, one for each index of `groups`. A program takes and returns all parts, laid end to end along the dimension named above; an argument that names none is the same for every part. Nothing has to cross between parts.
All inputs are finite; a program needn't handle non-finite values.
Results may differ from a plain program's by a relative error of at most 0.005.
Values may be sent and summed in bfloat16 or wider, within the bound.
No kernel may reach another device: no remote copies, remote signals or barrier semaphores. Data moves between devices by JAX's collectives and lax.ppermute only.
A program may use at most 64 MiB of HBM per device.

v0:
```python
import math
import jax
import numpy as np
import jax.numpy as jnp
from jax import lax
from jax.sharding import PartitionSpec as P

lag_group = 4


def toeplitz_blocks(windows, block_rows):
    flipped = windows[..., ::-1]
    tiled = jnp.tile(flipped, (1, 1, block_rows))
    trimmed = tiled[..., : block_rows * (2 * block_rows - 1)]
    shaped = trimmed.reshape(windows.shape[0], windows.shape[1], block_rows, 2 * block_rows - 1)
    return shaped[..., block_rows - 1 : 2 * block_rows - 1]


def diagonal_sums(products, block_rows):
    flipped = products[..., ::-1]
    padded = jnp.pad(flipped, ((0, 0), (0, 0), (0, 0), (0, block_rows)))
    flattened = padded.reshape(products.shape[0], products.shape[1], 2 * block_rows * block_rows)
    trimmed = flattened[..., : block_rows * (2 * block_rows - 1)]
    shaped = trimmed.reshape(products.shape[0], products.shape[1], block_rows, 2 * block_rows - 1)
    diag_sums = jnp.sum(shaped, axis=2)
    return jnp.pad(diag_sums, ((0, 0), (0, 0), (1, 0)))


def fold_windows(window_grads, block_rows):
    front_half = jnp.pad(window_grads[..., :block_rows], ((0, 1), (0, 0), (0, 0)))
    back_half = jnp.pad(window_grads[..., block_rows:], ((1, 0), (0, 0), (0, 0)))
    joined = front_half + back_half
    return jnp.transpose(joined, (1, 0, 2)).reshape(window_grads.shape[1], -1)


def lag_table(taps_all, block_rows):
    return jnp.pad(jnp.transpose(taps_all), ((0, 0), (block_rows, lag_group * block_rows)))


def lag_sweep(
    blocks, base_block, block_count, sources, tap_table, block_rows, trip_count, seq_count
):
    filters = sources.shape[2]
    group_width = sources.shape[3]

    def advance(lag_step, state_pair):
        input_acc, lag_acc = state_pair
        lag_start = lag_step * lag_group
        stacked = jnp.stack(
            [
                lax.dynamic_slice_in_dim(blocks, base_block + lag_start + offset, block_count, 0)
                for offset in range(lag_group)
            ],
            axis=1,
        )
        lag_span = lax.dynamic_slice_in_dim(
            tap_table, lag_start * block_rows, (lag_group + 1) * block_rows, 1
        )
        windows = jnp.stack(
            [
                lag_span[:, offset * block_rows : (offset + 2) * block_rows]
                for offset in range(lag_group)
            ],
            axis=0,
        )
        toeplitz = toeplitz_blocks(windows, block_rows)
        input_acc = input_acc + jnp.einsum(
            "kfts,iktfg->isfg", toeplitz, stacked, preferred_element_type=jnp.float32
        )
        products = jnp.einsum(
            "iktfg,isfg->kfts", stacked, sources, preferred_element_type=jnp.float32
        )
        folded = fold_windows(diagonal_sums(products, block_rows), block_rows)
        previous = lax.dynamic_slice_in_dim(
            lag_acc, lag_start * block_rows, (lag_group + 1) * block_rows, 1
        )
        lag_acc = lax.dynamic_update_slice_in_dim(
            lag_acc, previous + folded, lag_start * block_rows, 1
        )
        return (input_acc, lag_acc)

    initial = (
        jnp.zeros((block_count, block_rows, filters, group_width), jnp.float32),
        jnp.zeros((filters, (seq_count + 1 + lag_group) * block_rows), jnp.float32),
    )
    return lax.fori_loop(0, trip_count, advance, initial)


def per_device(cached_input, cached_gate, out_grad, filter_taps, skip_gain):
    block_rows = cached_input.shape[0]
    chan_width = cached_input.shape[1]
    filters = filter_taps.shape[1]
    group_width = chan_width // filters
    seq_count = lax.axis_size("seq")
    seq_index = lax.axis_index("seq")
    length = block_rows * seq_count
    taps_scale = 1.0 / math.sqrt(length)
    gated_grad = (out_grad.astype(jnp.float32) * cached_gate.astype(jnp.float32)).astype(
        jnp.bfloat16
    )
    stretch_width = chan_width // seq_count
    stretch_filters = max(1, stretch_width // group_width)
    stretch_group = stretch_width // stretch_filters
    first_filter = seq_index * stretch_width // group_width
    tap_columns = np.array(
        [
            target * stretch_width // group_width + offset
            for target in range(seq_count)
            for offset in range(stretch_filters)
        ]
    )
    routed_taps = filter_taps[:, tap_columns].reshape(block_rows, seq_count, stretch_filters)
    packed = jnp.concatenate(
        [
            gated_grad.reshape(block_rows, seq_count, stretch_width),
            cached_input.reshape(block_rows, seq_count, stretch_width),
            routed_taps,
        ],
        axis=2,
    )
    moved = lax.all_to_all(packed, "seq", split_axis=1, concat_axis=0, tiled=True)
    moved = moved.reshape(length, 2 * stretch_width + stretch_filters)
    moved_grad = moved[:, :stretch_width]
    moved_input = moved[:, stretch_width : 2 * stretch_width]
    stretch_taps = moved[:, 2 * stretch_width :]
    shaped_grad = moved_grad.reshape(seq_count, block_rows, stretch_filters, stretch_group)
    blocks = jnp.pad(shaped_grad, ((0, seq_count - 1 + lag_group), (0, 0), (0, 0), (0, 0)))
    sources = moved_input.reshape(seq_count, block_rows, stretch_filters, stretch_group)
    trip_count = (seq_count + lag_group - 1) // lag_group
    input_acc, lag_acc = lag_sweep(
        blocks,
        0,
        seq_count,
        sources,
        lag_table(stretch_taps, block_rows),
        block_rows,
        trip_count,
        seq_count,
    )
    stretch_gain = lax.dynamic_slice_in_dim(skip_gain, seq_index * stretch_width, stretch_width, 0)
    conv_grad = input_acc.reshape(length, stretch_width) * taps_scale
    local_grad = (conv_grad + stretch_gain[None, :] * moved_grad.astype(jnp.float32)).astype(
        jnp.bfloat16
    )
    input_grad = lax.all_to_all(local_grad, "seq", split_axis=0, concat_axis=1, tiled=True)
    stretch_term = jnp.transpose(lag_acc[:, block_rows : block_rows + length]) * taps_scale
    lag_parts = lax.all_to_all(
        stretch_term.reshape(seq_count, block_rows, stretch_filters),
        "seq",
        split_axis=0,
        concat_axis=0,
        tiled=True,
    )
    sharers = seq_count * stretch_filters // filters
    filter_grad = (
        jnp.transpose(lag_parts, (1, 0, 2)).reshape(block_rows, filters, sharers).sum(axis=2)
    )
    return (input_grad, filter_grad)


def solution(mesh):
    return jax.shard_map(
        per_device,
        mesh=mesh,
        in_specs=(
            P(("groups", "seq"), "chan"),
            P(("groups", "seq"), "chan"),
            P(("groups", "seq"), "chan"),
            P("seq", "chan"),
            P("chan"),
        ),
        out_specs=(P(("groups", "seq"), "chan"), P(("groups", "seq"), "chan")),
        check_vma=False,
    )
```

profile of v0, /device:TPU:0, one launch (start us, length us, event | category | flops | bytes accessed | tf_op | source)
XLA Modules:
  0.0 98.7 jit_solution(5453652676311803673)
XLA Ops:
  0.6 0.0 copy-start
  0.6 0.0 copy-start.4
  0.7 0.0 copy-start.5
  0.7 1.4 %copy.32 = bf16[128,2048]{0,1:T(8,128)(2,1)S(1)} copy(bf16[128,2048]{1,0:T(8,128)(2,1)} %param.9) | data formatting | bytes 1048576 | tf_op args[0]
  2.1 0.0 copy-done.4
  2.1 0.0 copy-done.5
  2.1 0.1 multiply_convert_fusion
  2.2 0.3 copy.31
  2.5 0.6 gather_fusion
  3.1 1.1 %pad_maximum_fusion.4 = bf16[128,8,514]{0,2,1:T(8,128)(2,1)} fusion(bf16[128,8,2]{0,2,1:T(2,128)(2,1)S(1)} %bitcast.138, bf16[128,8,256]{0,2,1:T(8,128)(2,1)S(1)} %bitcast.136, bf16[128,8,256]{0,2,1:T(8,128)(2,1)S(1)} %bitcast.137), kind=kLoop, calls=%fused_computation.25 | loop fusion | flops 3158016 | bytes 2105344 | tf_op jit(solution)/shard_map/concatenate | solution.py:113
  4.2 7.3 %all-to-all-start = ((bf16[128,8,514]{0,2,1:T(8,128)(2,1)}), bf16[128,8,514]{0,2,1:T(8,128)(2,1)S(1)}, u32[]{:S(2)}, u32[]{:S(2)}) async-start(bf16[128,8,514]{0,2,1:T(8,128)(2,1)} %pad_maximum_fusion.4), calls=%async_computation | async-start | bytes 2129920 | tf_op jit(solution)/shard_map/all_to_all | solution.py:121
  11.4 0.8 dynamic_slice.63
  12.2 25.4 %all-to-all-done = bf16[128,8,514]{0,2,1:T(8,128)(2,1)S(1)} async-done(((bf16[128,8,514]{0,2,1:T(8,128)(2,1)}), bf16[128,8,514]{0,2,1:T(8,128)(2,1)S(1)}, u32[]{:S(2)}, u32[]{:S(2)}) %all-to-all-start) | async-done | bytes 1052704 | tf_op jit(solution)/shard_map/all_to_all | solution.py:121
  37.6 0.1 copy.63
  37.7 0.1 pad.70
  37.8 0.3 copy.51
  38.1 0.1 slice_bitcast_fusion
  38.2 0.1 copy.52
  38.3 0.8 copy-done.3
  39.1 0.1 copy.34
  39.2 0.2 pad.52
  39.4 0.1 copy.53
  39.5 1.1 %copy.35 = bf16[8,128,2,128]{3,1,0,2:T(8,128)(2,1)} copy(bf16[8,128,2,128]{1,0,3,2:T(8,128)(2,1)S(1)} %bitcast.135) | data formatting | bytes 1048576
  40.6 26.8 %while.18 = (s32[]{:T(128)}, f32[8,128,2,128]{1,3,0,2:T(8,128)}, f32[2,1664]{1,0:T(2,128)S(1)}, bf16[19,128,2,128]{1,3,0,2:T(8,128)(2,1)S(1)}, bf16[2,1664]{1,0:...) while((s32[]{:T(128)}, f32[8,128,2,128]{1,3,0,2:T(8,128)}, ...), condition=%wide.region_2.3_spmd.clone, body=%wide.region_0.2_spmd.clone.sunk | while | flops 543954432 | bytes 31783416 | solution.py:86
  40.6 1.2 %dynamic-slice_bitcast_fusion.5 = (bf16[8,1,128,2,128]{2,4,1,0,3:T(8,128)(2,1)S(1)}, bf16[8,1,128,2,128]{2,4,1,0,3:T(8,128)(2,1)S(1)}, bf16[8,1,128,2,128]{2,4,1,0,3:T(8,128)(2,1)}, bf16[8,1,128,2,128]{2,4,1,0,3:T(8,128)(2,1)}) fusion(bf16[19,128,2,128]{1,3,0,2:T(8,128)(2,1)S(1)} %get-tuple-element.324, s32[]{:T(128)S(6)} %select_n.70, ...), kind=kLoop, calls=%fused_computation.9.clone.1 | loop fusion | bytes 4194320 | tf_op jit(solution)/shard_map/while/body/eval_jaxpr/stack | solution.py:49
  41.8 0.2 rev.24
  42.1 0.1 tile.29
  42.2 0.4 slice.144
  42.6 1.6 %reshape.107 = bf16[4,2,128,255]{3,2,1,0:T(8,128)(2,1)S(1)} reshape(bf16[4,2,32640]{2,1,0:T(2,128)(2,1)S(1)} %slice.144) | data formatting | bytes 1044480 | tf_op jit(solution)/shard_map/while/body/eval_jaxpr/reshape | solution.py:15
  44.2 0.0 copy-start.6
  44.2 3.1 %fusion.21 = f32[8,128,2,128]{1,3,0,2:T(8,128)} fusion(f32[8,128,2,128]{1,3,0,2:T(8,128)} %get-tuple-element.301, pred[]{:T(512)S(6)} %compare.9, bf16[8,1,128,2,128]{2,4,1,0,3:T(8,128)(2,1)S(1)} %get-tuple-element.269, bf16[8,1,128,2,128]{2,4,1,0,3:T(8,128)(2,1)} %get-tuple-element.270, bf16[8,1,128,2,128]{2,4,1,0,3:T(8,128)(2,1)} %get-tuple-element.271, ...), kind=kOutput, calls=%fused_computation.3.clone.1 | convolution fusion | flops 272105472 | bytes 4456449 | tf_op jit(solution)/shard_map/while/body/eval_jaxpr/kfts,iktfg->isfg/dot_general | solution.py:67
  47.3 1.1 %convolution_bitcast_fusion.3 = f32[4,2,128,128]{3,2,0,1:T(8,128)S(1)} fusion(bf16[8,128,2,128]{3,1,0,2:T(8,128)(2,1)S(1)} %copy-done.6, bf16[8,1,128,2,128]{2,4,1,0,3:T(8,128)(2,1)S(1)} %get-tuple-element.269, bf16[8,1,128,2,128]{2,4,1,0,3:T(8,128)(2,1)S(1)} %copy-done.1, bf16[8,1,128,2,128]{2,4,1,0,3:T(8,128)(2,1)S(1)} %copy-done.2, ...), kind=kOutput, calls=%fused_computation.4.clone.1 | convolution fusion | flops 271581184 | bytes 3145728 | tf_op jit(solution)/shard_map/while/body/eval_jaxpr/iktfg,isfg->kfts/dot_general | solution.py:70
  48.4 0.7 rev.25
  49.1 0.1 pad.125
  49.3 0.5 reshape.108
  49.8 1.0 %slice.145 = f32[4,2,32640]{2,0,1:T(4,128)} slice(f32[4,2,32768]{2,0,1:T(4,128)S(1)} %reshape.108), slice={[0:4], [0:2], [0:32640]} | slice | bytes 2088960 | tf_op jit(solution)/shard_map/while/body/eval_jaxpr/slice | solution.py:23
  50.8 2.8 %reshape.109 = f32[4,2,128,255]{3,2,0,1:T(8,128)S(1)} reshape(f32[4,2,32640]{2,0,1:T(4,128)} %slice.145) | data formatting | bytes 2088960 | tf_op jit(solution)/shard_map/while/body/eval_jaxpr/reshape | solution.py:24
  53.6 0.1 reduce_sum.25
  53.7 0.1 pad_slice_fusion.2
  53.9 1.2 %dynamic-slice_bitcast_fusion.5 = (bf16[8,1,128,2,128]{2,4,1,0,3:T(8,128)(2,1)S(1)}, bf16[8,1,128,2,128]{2,4,1,0,3:T(8,128)(2,1)S(1)}, bf16[8,1,128,2,128]{2,4,1,0,3:T(8,128)(2,1)}, bf16[8,1,128,2,128]{2,4,1,0,3:T(8,128)(2,1)}) fusion(bf16[19,128,2,128]{1,3,0,2:T(8,128)(2,1)S(1)} %get-tuple-element.324, s32[]{:T(128)S(6)} %select_n.70, ...), kind=kLoop, calls=%fused_computation.9.clone.1 | loop fusion | bytes 4194320 | tf_op jit(solution)/shard_map/while/body/eval_jaxpr/stack | solution.py:49
  55.1 0.2 rev.24
  55.3 0.1 tile.29
  55.5 0.4 slice.144
  55.8 1.6 %reshape.107 = bf16[4,2,128,255]{3,2,1,0:T(8,128)(2,1)S(1)} reshape(bf16[4,2,32640]{2,1,0:T(2,128)(2,1)S(1)} %slice.144) | data formatting | bytes 1044480 | tf_op jit(solution)/shard_map/while/body/eval_jaxpr/reshape | solution.py:15
  57.4 0.0 copy-start.6
  57.4 3.5 %fusion.21 = f32[8,128,2,128]{1,3,0,2:T(8,128)} fusion(f32[8,128,2,128]{1,3,0,2:T(8,128)} %get-tuple-element.301, pred[]{:T(512)S(6)} %compare.9, bf16[8,1,128,2,128]{2,4,1,0,3:T(8,128)(2,1)S(1)} %get-tuple-element.269, bf16[8,1,128,2,128]{2,4,1,0,3:T(8,128)(2,1)} %get-tuple-element.270, bf16[8,1,128,2,128]{2,4,1,0,3:T(8,128)(2,1)} %get-tuple-element.271, ...), kind=kOutput, calls=%fused_computation.3.clone.1 | convolution fusion | flops 272105472 | bytes 4456449 | tf_op jit(solution)/shard_map/while/body/eval_jaxpr/kfts,iktfg->isfg/dot_general | solution.py:67
  60.9 1.1 %convolution_bitcast_fusion.3 = f32[4,2,128,128]{3,2,0,1:T(8,128)S(1)} fusion(bf16[8,128,2,128]{3,1,0,2:T(8,128)(2,1)S(1)} %copy-done.6, bf16[8,1,128,2,128]{2,4,1,0,3:T(8,128)(2,1)S(1)} %get-tuple-element.269, bf16[8,1,128,2,128]{2,4,1,0,3:T(8,128)(2,1)S(1)} %copy-done.1, bf16[8,1,128,2,128]{2,4,1,0,3:T(8,128)(2,1)S(1)} %copy-done.2, ...), kind=kOutput, calls=%fused_computation.4.clone.1 | convolution fusion | flops 271581184 | bytes 3145728 | tf_op jit(solution)/shard_map/while/body/eval_jaxpr/iktfg,isfg->kfts/dot_general | solution.py:70
  62.0 0.7 rev.25
  62.8 0.1 pad.125
  62.9 0.5 reshape.108
  63.4 1.0 %slice.145 = f32[4,2,32640]{2,0,1:T(4,128)} slice(f32[4,2,32768]{2,0,1:T(4,128)S(1)} %reshape.108), slice={[0:4], [0:2], [0:32640]} | slice | bytes 2088960 | tf_op jit(solution)/shard_map/while/body/eval_jaxpr/slice | solution.py:23
  64.4 2.8 %reshape.109 = f32[4,2,128,255]{3,2,0,1:T(8,128)S(1)} reshape(f32[4,2,32640]{2,0,1:T(4,128)} %slice.145) | data formatting | bytes 2088960 | tf_op jit(solution)/shard_map/while/body/eval_jaxpr/reshape | solution.py:24
  67.3 0.1 reduce_sum.25
  67.4 0.1 pad_slice_fusion.2
  67.5 1.3 %broadcast_multiply_fusion = f32[8,128,2,128]{1,3,0,2:T(8,128)S(1)} fusion(f32[8,128,2,128]{1,3,0,2:T(8,128)} %get-tuple-element.161), kind=kLoop, calls=%fused_computation.33 | loop fusion | flops 262144 | bytes 2097152 | tf_op jit(solution)/shard_map/mul | solution.py:141
  68.8 0.6 copy.36
  69.4 0.6 multiply_bitcast_fusion
  70.0 3.6 %all-to-all-start.2 = ((f32[8,128,2]{1,2,0:T(2,128)}), f32[8,128,2]{1,2,0:T(2,128)S(1)}, u32[]{:S(2)}, u32[]{:S(2)}) async-start(f32[8,128,2]{1,2,0:T(2,128)} %multiply_bitcast_fusion), calls=%async_computation.2 | async-start | bytes 16384 | tf_op jit(solution)/shard_map/all_to_all | solution.py:147
  73.6 2.1 %copy_bitcast_fusion.3 = bf16[8,128,256]{1,2,0:T(8,128)(2,1)} fusion(f32[32,8,8,128]{3,2,1,0:T(8,128)S(1)} %bitcast.132, f32[256]{0:T(256)S(1)} %dynamic_slice.63, bf16[1024,514]{0,1:T(8,128)(2,1)} %bitcast.128), kind=kLoop, calls=%fused_computation.31 | loop fusion | flops 1048576 | bytes 2098176 | tf_op jit(solution)/shard_map/all_to_all | solution.py:145
  75.7 4.4 %all-to-all-done.2 = f32[8,128,2]{1,2,0:T(2,128)S(1)} async-done(((f32[8,128,2]{1,2,0:T(2,128)}), f32[8,128,2]{1,2,0:T(2,128)S(1)}, u32[]{:S(2)}, u32[]{:S(2)}) %all-to-all-start.2) | async-done | bytes 8224 | tf_op jit(solution)/shard_map/all_to_all | solution.py:147
  80.1 3.5 %all-to-all-start.1 = ((bf16[8,128,256]{1,2,0:T(8,128)(2,1)}), bf16[8,128,256]{1,2,0:T(8,128)(2,1)S(1)}, u32[]{:S(2)}, u32[]{:S(2)}) async-start(bf16[8,128,256]{1,2,0:T(8,128)(2,1)} %copy_bitcast_fusion.3), calls=%async_computation.1 | async-start | bytes 1048576 | tf_op jit(solution)/shard_map/all_to_all | solution.py:145
  83.6 13.4 %all-to-all-done.1 = bf16[8,128,256]{1,2,0:T(8,128)(2,1)S(1)} async-done(((bf16[8,128,256]{1,2,0:T(8,128)(2,1)}), bf16[8,128,256]{1,2,0:T(8,128)(2,1)S(1)}, u32[]{:S(2)}, u32[]{:S(2)}) %all-to-all-start.1) | async-done | bytes 524320 | tf_op jit(solution)/shard_map/all_to_all | solution.py:145
  97.1 1.0 %copy.39 = bf16[128,2048]{1,0:T(8,128)(2,1)} copy(bf16[128,2048]{0,1:T(8,128)(2,1)S(1)} %bitcast.133) | data formatting | bytes 1048576
  98.1 0.6 copy.79
  (28 shorter events, 0.2 us)
Async XLA Ops:
  0.6 1.9 %copy-start = (bf16[128,16]{0,1:T(8,128)(2,1)S(1)}, bf16[128,16]{0,1:T(8,128)(2,1)}, u32[]{:S(2)}) copy-start(bf16[128,16]{0,1:T(8,128)(2,1)} %param.12) | copy-start | bytes 12292
  0.6 1.4 %copy-start.4 = (bf16[128,2048]{1,0:T(8,128)(2,1)S(1)}, bf16[128,2048]{1,0:T(8,128)(2,1)}, u32[]{:S(2)}) copy-start(bf16[128,2048]{1,0:T(8,128)(2,1)} %param.10) | copy-start | bytes 1572868
  0.7 1.4 %copy-start.5 = (bf16[128,2048]{1,0:T(8,128)(2,1)S(1)}, bf16[128,2048]{1,0:T(8,128)(2,1)}, u32[]{:S(2)}) copy-start(bf16[128,2048]{1,0:T(8,128)(2,1)} %param.11) | copy-start | bytes 1572868
  4.2 33.4 %all-to-all-start = ((bf16[128,8,514]{0,2,1:T(8,128)(2,1)}), bf16[128,8,514]{0,2,1:T(8,128)(2,1)S(1)}, u32[]{:S(2)}, u32[]{:S(2)}) async-start(bf16[128,8,514]{0,2,1:T(8,128)(2,1)} %pad_maximum_fusion.4), calls=%async_computation | async-start | bytes 2129920 | tf_op jit(solution)/shard_map/all_to_all | solution.py:121
  38.1 1.0 copy-start.3
  44.1 3.2 %copy-start.1 = (bf16[8,1,128,2,128]{2,4,1,0,3:T(8,128)(2,1)S(1)}, bf16[8,1,128,2,128]{2,4,1,0,3:T(8,128)(2,1)}, u32[]{:S(2)}) copy-start(bf16[8,1,128,2,128]{2,4,1,0,3:T(8,128)(2,1)} %get-tuple-element.270) | copy-start | bytes 1572868 | tf_op jit(solution)/shard_map/while
  44.1 3.2 %copy-start.2 = (bf16[8,1,128,2,128]{2,4,1,0,3:T(8,128)(2,1)S(1)}, bf16[8,1,128,2,128]{2,4,1,0,3:T(8,128)(2,1)}, u32[]{:S(2)}) copy-start(bf16[8,1,128,2,128]{2,4,1,0,3:T(8,128)(2,1)} %get-tuple-element.271) | copy-start | bytes 1572868 | tf_op jit(solution)/shard_map/while
  44.2 3.1 %copy-start.6 = (bf16[8,128,2,128]{3,1,0,2:T(8,128)(2,1)S(1)}, bf16[8,128,2,128]{3,1,0,2:T(8,128)(2,1)}, u32[]{:S(2)}) copy-start(bf16[8,128,2,128]{3,1,0,2:T(8,128)(2,1)} %get-tuple-element.326) | copy-start | bytes 1572868 | tf_op jit(solution)/shard_map/while
  57.4 3.5 %copy-start.1 = (bf16[8,1,128,2,128]{2,4,1,0,3:T(8,128)(2,1)S(1)}, bf16[8,1,128,2,128]{2,4,1,0,3:T(8,128)(2,1)}, u32[]{:S(2)}) copy-start(bf16[8,1,128,2,128]{2,4,1,0,3:T(8,128)(2,1)} %get-tuple-element.270) | copy-start | bytes 1572868 | tf_op jit(solution)/shard_map/while
  57.4 3.5 %copy-start.2 = (bf16[8,1,128,2,128]{2,4,1,0,3:T(8,128)(2,1)S(1)}, bf16[8,1,128,2,128]{2,4,1,0,3:T(8,128)(2,1)}, u32[]{:S(2)}) copy-start(bf16[8,1,128,2,128]{2,4,1,0,3:T(8,128)(2,1)} %get-tuple-element.271) | copy-start | bytes 1572868 | tf_op jit(solution)/shard_map/while
  57.4 3.5 %copy-start.6 = (bf16[8,128,2,128]{3,1,0,2:T(8,128)(2,1)S(1)}, bf16[8,128,2,128]{3,1,0,2:T(8,128)(2,1)}, u32[]{:S(2)}) copy-start(bf16[8,128,2,128]{3,1,0,2:T(8,128)(2,1)} %get-tuple-element.326) | copy-start | bytes 1572868 | tf_op jit(solution)/shard_map/while
  70.0 10.1 %all-to-all-start.2 = ((f32[8,128,2]{1,2,0:T(2,128)}), f32[8,128,2]{1,2,0:T(2,128)S(1)}, u32[]{:S(2)}, u32[]{:S(2)}) async-start(f32[8,128,2]{1,2,0:T(2,128)} %multiply_bitcast_fusion), calls=%async_computation.2 | async-start | bytes 16384 | tf_op jit(solution)/shard_map/all_to_all | solution.py:147
  80.1 16.9 %all-to-all-start.1 = ((bf16[8,128,256]{1,2,0:T(8,128)(2,1)}), bf16[8,128,256]{1,2,0:T(8,128)(2,1)S(1)}, u32[]{:S(2)}, u32[]{:S(2)}) async-start(bf16[8,128,256]{1,2,0:T(8,128)(2,1)} %copy_bitcast_fusion.3), calls=%async_computation.1 | async-start | bytes 1048576 | tf_op jit(solution)/shard_map/all_to_all | solution.py:145
where the time goes:
time: 99.2 us; the launch traced here: 98.7 us
  waiting for transfers between devices  43.2 us (44%)
  local copies, waits for them, and re-layouts  25.7 us (26%)
  starting transfers between devices  14.4 us (15%)
  matrix products  8.83 us (9%)
  other arithmetic  5.49 us (6%)
    all_to_all x1, waiting for transfers between devices, per_device(): lax.all_to_all(packed, 'seq', split_axis=1, concat_axis=0, tiled=True)  25.4 us
    all_to_all x1, waiting for transfers between devices, per_device(): lax.all_to_all(local_grad, 'seq', split_axis=0, concat_axis=1, tiled=True)  13.4 us
    all_to_all x1, starting transfers between devices, per_device(): lax.all_to_all(packed, 'seq', split_axis=1, concat_axis=0, tiled=True)  7.28 us
    dot_general x2, matrix products, advance(): jnp.einsum('kfts,iktfg->isfg', toeplitz, stacked, preferred_element_type=...  6.6 us
    reshape x2, local copies, waits for them, and re-layouts, diagonal_sums(): trimmed.reshape(products.shape[0], products.shape[1], block_rows, 2 * blo...  5.62 us
    unnamed x17, local copies, waits for them, and re-layouts  5.54 us
    all_to_all x1, waiting for transfers between devices, per_device(): lax.all_to_all(stretch_term.reshape(seq_count, block_rows, stretch_filter...  4.37 us
    all_to_all x1, starting transfers between devices, per_device(): lax.all_to_all(stretch_term.reshape(seq_count, block_rows, stretch_filter...  3.59 us
  transfers between devices with their start and end apart: 3, of which 3 were waited for; matrix products, arithmetic and copies ran while one was open for 3% of the time, Pallas kernels for 0%

commit v1 on v0

--- a/solution.py
+++ b/solution.py
@@ -6,6 +6,29 @@
 from jax.sharding import PartitionSpec as P
 
 lag_group = 4
+
+
+def split_up(x, dim, size):
+    dims = x.shape
+    pieces = x.reshape(*dims[:dim], size, dims[dim] // size, *dims[dim + 1 :])
+    return jnp.moveaxis(pieces, dim, 0)
+
+
+def in_order(blocks, dim):
+    lengths = list(blocks.shape[1:])
+    lengths[dim] *= blocks.shape[0]
+    return jnp.moveaxis(blocks, 0, dim).reshape(lengths)
+
+
+def sent_to_each(x, axis, split_dim, concat_dim):
+    size, mine = (lax.axis_size(axis), lax.axis_index(axis))
+    tiles = split_up(x, split_dim, size)
+    outs = [tiles[mine]]
+    for step in range(1, size):
+        sent = tiles[(mine + step) % size]
+        outs.append(lax.ppermute(sent, axis, [(i, (i + step) % size) for i in range(size)]))
+    tiles = jnp.stack(outs)[(mine - jnp.arange(size)) % size]
+    return in_order(tiles, concat_dim)
 
 
 def toeplitz_blocks(windows, block_rows):
@@ -142,7 +165,7 @@
     local_grad = (conv_grad + stretch_gain[None, :] * moved_grad.astype(jnp.float32)).astype(
         jnp.bfloat16
     )
-    input_grad = lax.all_to_all(local_grad, "seq", split_axis=0, concat_axis=1, tiled=True)
+    input_grad = sent_to_each(local_grad, "seq", 0, 1)
     stretch_term = jnp.transpose(lag_acc[:, block_rows : block_rows + length]) * taps_scale
     lag_parts = lax.all_to_all(
         stretch_term.reshape(seq_count, block_rows, stretch_filters),

time: 99.2 us -> 94.8 us (0.956)
  waiting for transfers between devices: 43.2 us -> 28.1 us
  starting transfers between devices: 14.4 us -> 24.6 us
  local copies, waits for them, and re-layouts: 25.7 us -> 27 us
    all_to_all x1 -> x0, waiting for transfers between devices: 13.4 us -> none  [per_device(): lax.all_to_all(local_grad, 'seq', split_axis=0, concat_axis=1, tiled=True)]
    ppermute x0 -> x7, starting transfers between devices: none -> 12.7 us  [sent_to_each(): lax.ppermute(sent, axis, [(i, (i + step) % size) for i in range(size)])]
    all_to_all x1, waiting for transfers between devices: 4.37 us -> 0.01 us  [per_device(): lax.all_to_all(stretch_term.reshape(seq_count, block_rows, stretch_filter...]
    all_to_all x1 -> x0, starting transfers between devices: 3.49 us -> none  [per_device(): lax.all_to_all(local_grad, 'seq', split_axis=0, concat_axis=1, tiled=True)]
    ppermute x0 -> x7, waiting for transfers between devices: none -> 2.75 us  [sent_to_each(): lax.ppermute(sent, axis, [(i, (i + step) % size) for i in range(size)])]
    all_to_all x1 -> x0, other arithmetic: 2.14 us -> none  [per_device(): lax.all_to_all(local_grad, 'seq', split_axis=0, concat_axis=1, tiled=True)]
    convert_element_type x0 -> x1, other arithmetic: none -> 1.32 us  [per_device(): (conv_grad + stretch_gain[None, :] * moved_grad.astype(jnp.float32)).asty...]
    unnamed x17 -> x23, local copies, waits for them, and re-layouts: 5.54 us -> 5.6 us
  transfers between devices with their start and end apart: 3 -> 9, of which waited for: 3 -> 4; matrix products, arithmetic and copies ran while one was open for 3% -> 1% of each run, Pallas kernels for 0% -> 0%
where the time goes in v1:
time: 94.8 us; the launch traced here: 94.3 us
  waiting for transfers between devices  28.1 us (30%)
  local copies, waits for them, and re-layouts  27 us (28%)
  starting transfers between devices  24.6 us (26%)
  matrix products  8.8 us (9%)
  other arithmetic  4.7 us (5%)
    all_to_all x1, waiting for transfers between devices, per_device(): lax.all_to_all(packed, 'seq', split_axis=1, concat_axis=0, tiled=True)  25.3 us
    ppermute x7, starting transfers between devices, sent_to_each(): lax.ppermute(sent, axis, [(i, (i + step) % size) for i in range(size)])  12.7 us
    all_to_all x1, starting transfers between devices, per_device(): lax.all_to_all(packed, 'seq', split_axis=1, concat_axis=0, tiled=True)  7.28 us
    dot_general x2, matrix products, advance(): jnp.einsum('kfts,iktfg->isfg', toeplitz, stacked, preferred_element_type=...  6.56 us
    reshape x2, local copies, waits for them, and re-layouts, diagonal_sums(): trimmed.reshape(products.shape[0], products.shape[1], block_rows, 2 * blo...  5.62 us
    unnamed x23, local copies, waits for them, and re-layouts  5.6 us
    all_to_all x1, starting transfers between devices, per_device(): lax.all_to_all(stretch_term.reshape(seq_count, block_rows, stretch_filter...  4.58 us
    reshape x2, local copies, waits for them, and re-layouts, toeplitz_blocks(): trimmed.reshape(windows.shape[0], windows.shape[1], block_rows, 2 * block...  3.14 us
  transfers between devices with their start and end apart: 9, of which 4 were waited for; matrix products, arithmetic and copies ran while one was open for 1% of the time, Pallas kernels for 0%

profile of v1, /device:TPU:0, one launch (start us, length us, event | category | flops | bytes accessed | tf_op | source)
XLA Modules:
  0.0 94.3 jit_solution(16122392944701335439)
XLA Ops:
  0.7 1.4 %copy.44 = bf16[128,2048]{0,1:T(8,128)(2,1)S(1)} copy(bf16[128,2048]{1,0:T(8,128)(2,1)} %param.9) | data formatting | bytes 1048576 | tf_op args[0]
  2.1 0.1 multiply_convert_fusion
  2.2 0.3 copy.43
  2.5 0.6 gather_fusion
  3.1 1.1 %pad_maximum_fusion.4 = bf16[128,8,514]{0,2,1:T(8,128)(2,1)} fusion(bf16[128,8,2]{0,2,1:T(2,128)(2,1)S(1)} %bitcast.162, bf16[128,8,256]{0,2,1:T(8,128)(2,1)S(1)} %bitcast.160, bf16[128,8,256]{0,2,1:T(8,128)(2,1)S(1)} %bitcast.161), kind=kLoop, calls=%fused_computation.26 | loop fusion | flops 3158016 | bytes 2105344 | tf_op jit(solution)/shard_map/concatenate | solution.py:136
  4.2 7.3 %all-to-all-start = ((bf16[128,8,514]{0,2,1:T(8,128)(2,1)}), bf16[128,8,514]{0,2,1:T(8,128)(2,1)S(1)}, u32[]{:S(2)}, u32[]{:S(2)}) async-start(bf16[128,8,514]{0,2,1:T(8,128)(2,1)} %pad_maximum_fusion.4), calls=%async_computation | async-start | bytes 2129920 | tf_op jit(solution)/shard_map/all_to_all | solution.py:144
  11.5 0.8 dynamic_slice.87
  12.2 25.3 %all-to-all-done = bf16[128,8,514]{0,2,1:T(8,128)(2,1)S(1)} async-done(((bf16[128,8,514]{0,2,1:T(8,128)(2,1)}), bf16[128,8,514]{0,2,1:T(8,128)(2,1)S(1)}, u32[]{:S(2)}, u32[]{:S(2)}) %all-to-all-start) | async-done | bytes 1052704 | tf_op jit(solution)/shard_map/all_to_all | solution.py:144
  37.6 0.1 copy.71
  37.8 0.3 copy.63
  38.2 0.1 copy.64
  38.3 0.8 copy-done.3
  39.1 0.1 copy.46
  39.2 0.2 pad.52
  39.4 0.1 copy.65
  39.5 1.1 %copy.47 = bf16[8,128,2,128]{3,1,0,2:T(8,128)(2,1)} copy(bf16[8,128,2,128]{1,0,3,2:T(8,128)(2,1)S(1)} %bitcast.158) | data formatting | bytes 1048576
  40.7 26.9 %while.18 = (s32[]{:T(128)}, f32[8,128,2,128]{1,3,0,2:T(8,128)}, f32[2,1664]{1,0:T(2,128)S(1)}, bf16[19,128,2,128]{1,3,0,2:T(8,128)(2,1)S(1)}, bf16[2,1664]{1,0:...) while((s32[]{:T(128)}, f32[8,128,2,128]{1,3,0,2:T(8,128)}, ...), condition=%wide.region_2.3_spmd.clone, body=%wide.region_0.2_spmd.clone.sunk | while | flops 543954432 | bytes 31783416 | solution.py:109
  40.7 1.2 %dynamic-slice_bitcast_fusion.12 = (bf16[8,1,128,2,128]{2,4,1,0,3:T(8,128)(2,1)S(1)}, bf16[8,1,128,2,128]{2,4,1,0,3:T(8,128)(2,1)S(1)}, bf16[8,1,128,2,128]{2,4,1,0,3:T(8,128)(2,1)}, bf16[8,1,128,2,128]{2,4,1,0,3:T(8,128)(2,1)}) fusion(bf16[19,128,2,128]{1,3,0,2:T(8,128)(2,1)S(1)} %get-tuple-element.340, s32[]{:T(128)S(6)} %select_n.173, ...), kind=kLoop, calls=%fused_computation.10.clone.1 | loop fusion | bytes 4194320 | tf_op jit(solution)/shard_map/while/body/eval_jaxpr/stack | solution.py:72
  41.9 0.2 rev.24
  42.1 0.1 tile.29
  42.3 0.4 slice.145
  42.6 1.6 %reshape.169 = bf16[4,2,128,255]{3,2,1,0:T(8,128)(2,1)S(1)} reshape(bf16[4,2,32640]{2,1,0:T(2,128)(2,1)S(1)} %slice.145) | data formatting | bytes 1044480 | tf_op jit(solution)/shard_map/while/body/eval_jaxpr/reshape | solution.py:38
  44.2 3.1 %fusion.21 = f32[8,128,2,128]{1,3,0,2:T(8,128)} fusion(f32[8,128,2,128]{1,3,0,2:T(8,128)} %get-tuple-element.317, pred[]{:T(512)S(6)} %compare.23, bf16[8,1,128,2,128]{2,4,1,0,3:T(8,128)(2,1)S(1)} %get-tuple-element.285, bf16[8,1,128,2,128]{2,4,1,0,3:T(8,128)(2,1)} %get-tuple-element.286, bf16[8,1,128,2,128]{2,4,1,0,3:T(8,128)(2,1)} %get-tuple-element.287, ...), kind=kOutput, calls=%fused_computation.4.clone.1 | convolution fusion | flops 272105472 | bytes 4456449 | tf_op jit(solution)/shard_map/while/body/eval_jaxpr/kfts,iktfg->isfg/dot_general | solution.py:90
  47.4 1.1 %convolution_bitcast_fusion.3 = f32[4,2,128,128]{3,2,0,1:T(8,128)S(1)} fusion(bf16[8,128,2,128]{3,1,0,2:T(8,128)(2,1)S(1)} %copy-done.6, bf16[8,1,128,2,128]{2,4,1,0,3:T(8,128)(2,1)S(1)} %get-tuple-element.285, bf16[8,1,128,2,128]{2,4,1,0,3:T(8,128)(2,1)S(1)} %copy-done.1, bf16[8,1,128,2,128]{2,4,1,0,3:T(8,128)(2,1)S(1)} %copy-done.2, ...), kind=kOutput, calls=%fused_computation.5.clone.1 | convolution fusion | flops 271581184 | bytes 3145728 | tf_op jit(solution)/shard_map/while/body/eval_jaxpr/iktfg,isfg->kfts/dot_general | solution.py:93
  48.5 0.7 rev.25
  49.2 0.1 pad.127
  49.3 0.5 reshape.170
  49.8 1.1 %slice.146 = f32[4,2,32640]{2,0,1:T(4,128)} slice(f32[4,2,32768]{2,0,1:T(4,128)S(1)} %reshape.170), slice={[0:4], [0:2], [0:32640]} | slice | bytes 2088960 | tf_op jit(solution)/shard_map/while/body/eval_jaxpr/slice | solution.py:46
  50.9 2.8 %reshape.171 = f32[4,2,128,255]{3,2,0,1:T(8,128)S(1)} reshape(f32[4,2,32640]{2,0,1:T(4,128)} %slice.146) | data formatting | bytes 2088960 | tf_op jit(solution)/shard_map/while/body/eval_jaxpr/reshape | solution.py:47
  53.7 0.1 reduce_sum.25
  53.8 0.1 pad_slice_fusion.2
  53.9 1.2 %dynamic-slice_bitcast_fusion.12 = (bf16[8,1,128,2,128]{2,4,1,0,3:T(8,128)(2,1)S(1)}, bf16[8,1,128,2,128]{2,4,1,0,3:T(8,128)(2,1)S(1)}, bf16[8,1,128,2,128]{2,4,1,0,3:T(8,128)(2,1)}, bf16[8,1,128,2,128]{2,4,1,0,3:T(8,128)(2,1)}) fusion(bf16[19,128,2,128]{1,3,0,2:T(8,128)(2,1)S(1)} %get-tuple-element.340, s32[]{:T(128)S(6)} %select_n.173, ...), kind=kLoop, calls=%fused_computation.10.clone.1 | loop fusion | bytes 4194320 | tf_op jit(solution)/shard_map/while/body/eval_jaxpr/stack | solution.py:72
  55.2 0.2 rev.24
  55.4 0.1 tile.29
  55.5 0.4 slice.145
  55.9 1.6 %reshape.169 = bf16[4,2,128,255]{3,2,1,0:T(8,128)(2,1)S(1)} reshape(bf16[4,2,32640]{2,1,0:T(2,128)(2,1)S(1)} %slice.145) | data formatting | bytes 1044480 | tf_op jit(solution)/shard_map/while/body/eval_jaxpr/reshape | solution.py:38
  57.5 3.5 %fusion.21 = f32[8,128,2,128]{1,3,0,2:T(8,128)} fusion(f32[8,128,2,128]{1,3,0,2:T(8,128)} %get-tuple-element.317, pred[]{:T(512)S(6)} %compare.23, bf16[8,1,128,2,128]{2,4,1,0,3:T(8,128)(2,1)S(1)} %get-tuple-element.285, bf16[8,1,128,2,128]{2,4,1,0,3:T(8,128)(2,1)} %get-tuple-element.286, bf16[8,1,128,2,128]{2,4,1,0,3:T(8,128)(2,1)} %get-tuple-element.287, ...), kind=kOutput, calls=%fused_computation.4.clone.1 | convolution fusion | flops 272105472 | bytes 4456449 | tf_op jit(solution)/shard_map/while/body/eval_jaxpr/kfts,iktfg->isfg/dot_general | solution.py:90
  61.0 1.1 %convolution_bitcast_fusion.3 = f32[4,2,128,128]{3,2,0,1:T(8,128)S(1)} fusion(bf16[8,128,2,128]{3,1,0,2:T(8,128)(2,1)S(1)} %copy-done.6, bf16[8,1,128,2,128]{2,4,1,0,3:T(8,128)(2,1)S(1)} %get-tuple-element.285, bf16[8,1,128,2,128]{2,4,1,0,3:T(8,128)(2,1)S(1)} %copy-done.1, bf16[8,1,128,2,128]{2,4,1,0,3:T(8,128)(2,1)S(1)} %copy-done.2, ...), kind=kOutput, calls=%fused_computation.5.clone.1 | convolution fusion | flops 271581184 | bytes 3145728 | tf_op jit(solution)/shard_map/while/body/eval_jaxpr/iktfg,isfg->kfts/dot_general | solution.py:93
  62.1 0.7 rev.25
  62.8 0.1 pad.127
  62.9 0.5 reshape.170
  63.5 1.1 %slice.146 = f32[4,2,32640]{2,0,1:T(4,128)} slice(f32[4,2,32768]{2,0,1:T(4,128)S(1)} %reshape.170), slice={[0:4], [0:2], [0:32640]} | slice | bytes 2088960 | tf_op jit(solution)/shard_map/while/body/eval_jaxpr/slice | solution.py:46
  64.5 2.8 %reshape.171 = f32[4,2,128,255]{3,2,0,1:T(8,128)S(1)} reshape(f32[4,2,32640]{2,0,1:T(4,128)} %slice.146) | data formatting | bytes 2088960 | tf_op jit(solution)/shard_map/while/body/eval_jaxpr/reshape | solution.py:47
  67.3 0.1 reduce_sum.25
  67.5 1.3 %broadcast_multiply_fusion = f32[8,128,2,128]{1,3,0,2:T(8,128)S(1)} fusion(f32[8,128,2,128]{1,3,0,2:T(8,128)} %get-tuple-element.161), kind=kLoop, calls=%fused_computation.32 | loop fusion | flops 262144 | bytes 2097152 | tf_op jit(solution)/shard_map/mul | solution.py:164
  68.9 0.6 copy.48
  69.5 1.3 %fusion.9 = bf16[1024,256]{0,1:T(8,128)(2,1)S(1)} fusion(f32[32,8,8,128]{3,2,1,0:T(8,128)S(1)} %bitcast.154, f32[256]{0:T(256)S(1)} %dynamic_slice.87, bf16[1024,514]{0,1:T(8,128)(2,1)} %bitcast.150), kind=kLoop, calls=%fused_computation.29 | loop fusion | flops 1048576 | bytes 2098176 | tf_op jit(solution)/shard_map/convert_element_type | solution.py:165
  70.8 0.2 copy.49
  71.1 1.5 %collective-permute-start = (bf16[128,256]{1,0:T(8,128)(2,1)S(1)}, bf16[128,256]{1,0:T(8,128)(2,1)S(1)}, u32[]{:S(2)}, u32[]{:S(2)}) collective-permute-start(bf16[128,256]{1,0:T(8,128)(2,1)S(1)} %get-tuple-element.236), channel_id=1, source_target_pairs={{0,2},{2,4},{4,6},{6,8},{8,10},{10,12},{12,14},{14,0},{1,3},{3,5},... | collective-permute-start | bytes 196616 | tf_op jit(solution)/shard_map/ppermute | solution.py:29
  72.5 0.6 multiply_bitcast_fusion
  73.2 4.6 %all-to-all-start.1 = ((f32[8,128,2]{1,2,0:T(2,128)}), f32[8,128,2]{1,2,0:T(2,128)S(1)}, u32[]{:S(2)}, u32[]{:S(2)}) async-start(f32[8,128,2]{1,2,0:T(2,128)} %multiply_bitcast_fusion), calls=%async_computation.1 | async-start | bytes 16384 | tf_op jit(solution)/shard_map/all_to_all | solution.py:170
  77.7 2.1 %collective-permute-start.1 = (bf16[128,256]{1,0:T(8,128)(2,1)S(1)}, bf16[128,256]{1,0:T(8,128)(2,1)S(1)}, u32[]{:S(2)}, u32[]{:S(2)}) collective-permute-start(bf16[128,256]{1,0:T(8,128)(2,1)S(1)} %get-tuple-element.235), channel_id=1, source_target_pairs={{0,4},{2,6},{4,8},{6,10},{8,12},{10,14},{12,0},{14,2},{1,5},{3,7},... | collective-permute-start | bytes 196616 | tf_op jit(solution)/shard_map/ppermute | solution.py:29
  79.8 2.4 %collective-permute-start.2 = (bf16[128,256]{1,0:T(8,128)(2,1)S(1)}, bf16[128,256]{1,0:T(8,128)(2,1)S(1)}, u32[]{:S(2)}, u32[]{:S(2)}) collective-permute-start(bf16[128,256]{1,0:T(8,128)(2,1)S(1)} %get-tuple-element.234), channel_id=1, source_target_pairs={{0,6},{2,8},{4,10},{6,12},{8,14},{10,0},{12,2},{14,4},{1,7},{3,9},... | collective-permute-start | bytes 196616 | tf_op jit(solution)/shard_map/ppermute | solution.py:29
  82.2 1.5 %collective-permute-start.3 = (bf16[128,256]{1,0:T(8,128)(2,1)S(1)}, bf16[128,256]{1,0:T(8,128)(2,1)S(1)}, u32[]{:S(2)}, u32[]{:S(2)}) collective-permute-start(bf16[128,256]{1,0:T(8,128)(2,1)S(1)} %get-tuple-element.233), channel_id=1, source_target_pairs={{0,8},{2,10},{4,12},{6,14},{8,0},{10,2},{12,4},{14,6},{1,9},{3,11}... | collective-permute-start | bytes 196616 | tf_op jit(solution)/shard_map/ppermute | solution.py:29
  83.6 2.4 %collective-permute-start.4 = (bf16[128,256]{1,0:T(8,128)(2,1)S(1)}, bf16[128,256]{1,0:T(8,128)(2,1)S(1)}, u32[]{:S(2)}, u32[]{:S(2)}) collective-permute-start(bf16[128,256]{1,0:T(8,128)(2,1)S(1)} %get-tuple-element.232), channel_id=1, source_target_pairs={{0,10},{2,12},{4,14},{6,0},{8,2},{10,4},{12,6},{14,8},{1,11},{3,13... | collective-permute-start | bytes 196616 | tf_op jit(solution)/shard_map/ppermute | solution.py:29
  86.0 1.5 %collective-permute-start.5 = (bf16[128,256]{1,0:T(8,128)(2,1)S(1)}, bf16[128,256]{1,0:T(8,128)(2,1)S(1)}, u32[]{:S(2)}, u32[]{:S(2)}) collective-permute-start(bf16[128,256]{1,0:T(8,128)(2,1)S(1)} %get-tuple-element.231), channel_id=1, source_target_pairs={{0,12},{2,14},{4,0},{6,2},{8,4},{10,6},{12,8},{14,10},{1,13},{3,15... | collective-permute-start | bytes 196616 | tf_op jit(solution)/shard_map/ppermute | solution.py:29
  87.5 1.5 %collective-permute-start.6 = (bf16[128,256]{1,0:T(8,128)(2,1)S(1)}, bf16[128,256]{1,0:T(8,128)(2,1)S(1)}, u32[]{:S(2)}, u32[]{:S(2)}) collective-permute-start(bf16[128,256]{1,0:T(8,128)(2,1)S(1)} %get-tuple-element.230), channel_id=1, source_target_pairs={{0,14},{2,0},{4,2},{6,4},{8,6},{10,8},{12,10},{14,12},{1,15},{3,1}... | collective-permute-start | bytes 196616 | tf_op jit(solution)/shard_map/ppermute | solution.py:29
  89.0 0.9 collective-permute-done.3
  90.0 0.8 collective-permute-done.5
  90.8 1.0 %collective-permute-done.6 = bf16[128,256]{1,0:T(8,128)(2,1)S(1)} collective-permute-done((bf16[128,256]{1,0:T(8,128)(2,1)S(1)}, bf16[128,256]{1,0:T(8,128)(2,1)S(1)}, u32[]{:S(2)}, u32[]{:S(2)}) %collective-permute-start.6) | collective-permute-done | bytes 65568 | tf_op jit(solution)/shard_map/ppermute | solution.py:29
  91.8 0.6 gather_fusion.1
  92.4 0.3 copy.50
  92.7 1.0 %copy.52 = bf16[128,2048]{1,0:T(8,128)(2,1)} copy(bf16[128,2048]{0,1:T(8,128)(2,1)S(1)} %bitcast.159) | data formatting | bytes 1048576
  93.7 0.6 copy.94
  (53 shorter events, 0.6 us)
Async XLA Ops:
  0.6 1.9 %copy-start = (bf16[128,16]{0,1:T(8,128)(2,1)S(1)}, bf16[128,16]{0,1:T(8,128)(2,1)}, u32[]{:S(2)}) copy-start(bf16[128,16]{0,1:T(8,128)(2,1)} %param.12) | copy-start | bytes 12292
  0.6 1.4 %copy-start.4 = (bf16[128,2048]{1,0:T(8,128)(2,1)S(1)}, bf16[128,2048]{1,0:T(8,128)(2,1)}, u32[]{:S(2)}) copy-start(bf16[128,2048]{1,0:T(8,128)(2,1)} %param.10) | copy-start | bytes 1572868
  0.7 1.4 %copy-start.5 = (bf16[128,2048]{1,0:T(8,128)(2,1)S(1)}, bf16[128,2048]{1,0:T(8,128)(2,1)}, u32[]{:S(2)}) copy-start(bf16[128,2048]{1,0:T(8,128)(2,1)} %param.11) | copy-start | bytes 1572868
  4.2 33.4 %all-to-all-start = ((bf16[128,8,514]{0,2,1:T(8,128)(2,1)}), bf16[128,8,514]{0,2,1:T(8,128)(2,1)S(1)}, u32[]{:S(2)}, u32[]{:S(2)}) async-start(bf16[128,8,514]{0,2,1:T(8,128)(2,1)} %pad_maximum_fusion.4), calls=%async_computation | async-start | bytes 2129920 | tf_op jit(solution)/shard_map/all_to_all | solution.py:144
  38.1 1.0 %copy-start.3 = (bf16[65,8,8,128]{3,1,2,0:T(8,128)(2,1)}, bf16[65,8,8,128]{3,1,2,0:T(8,128)(2,1)S(1)}, u32[]{:S(2)}) copy-start(bf16[65,8,8,128]{3,1,2,0:T(8,128)(2,1)S(1)} %copy.63) | copy-start | bytes 3194884
  44.2 3.1 %copy-start.1 = (bf16[8,1,128,2,128]{2,4,1,0,3:T(8,128)(2,1)S(1)}, bf16[8,1,128,2,128]{2,4,1,0,3:T(8,128)(2,1)}, u32[]{:S(2)}) copy-start(bf16[8,1,128,2,128]{2,4,1,0,3:T(8,128)(2,1)} %get-tuple-element.286) | copy-start | bytes 1572868 | tf_op jit(solution)/shard_map/while
  44.2 3.1 %copy-start.2 = (bf16[8,1,128,2,128]{2,4,1,0,3:T(8,128)(2,1)S(1)}, bf16[8,1,128,2,128]{2,4,1,0,3:T(8,128)(2,1)}, u32[]{:S(2)}) copy-start(bf16[8,1,128,2,128]{2,4,1,0,3:T(8,128)(2,1)} %get-tuple-element.287) | copy-start | bytes 1572868 | tf_op jit(solution)/shard_map/while
  44.2 3.1 %copy-start.6 = (bf16[8,128,2,128]{3,1,0,2:T(8,128)(2,1)S(1)}, bf16[8,128,2,128]{3,1,0,2:T(8,128)(2,1)}, u32[]{:S(2)}) copy-start(bf16[8,128,2,128]{3,1,0,2:T(8,128)(2,1)} %get-tuple-element.342) | copy-start | bytes 1572868 | tf_op jit(solution)/shard_map/while
  57.5 3.5 %copy-start.1 = (bf16[8,1,128,2,128]{2,4,1,0,3:T(8,128)(2,1)S(1)}, bf16[8,1,128,2,128]{2,4,1,0,3:T(8,128)(2,1)}, u32[]{:S(2)}) copy-start(bf16[8,1,128,2,128]{2,4,1,0,3:T(8,128)(2,1)} %get-tuple-element.286) | copy-start | bytes 1572868 | tf_op jit(solution)/shard_map/while
  57.5 3.5 %copy-start.2 = (bf16[8,1,128,2,128]{2,4,1,0,3:T(8,128)(2,1)S(1)}, bf16[8,1,128,2,128]{2,4,1,0,3:T(8,128)(2,1)}, u32[]{:S(2)}) copy-start(bf16[8,1,128,2,128]{2,4,1,0,3:T(8,128)(2,1)} %get-tuple-element.287) | copy-start | bytes 1572868 | tf_op jit(solution)/shard_map/while
  57.5 3.5 %copy-start.6 = (bf16[8,128,2,128]{3,1,0,2:T(8,128)(2,1)S(1)}, bf16[8,128,2,128]{3,1,0,2:T(8,128)(2,1)}, u32[]{:S(2)}) copy-start(bf16[8,128,2,128]{3,1,0,2:T(8,128)(2,1)} %get-tuple-element.342) | copy-start | bytes 1572868 | tf_op jit(solution)/shard_map/while
  71.1 14.9 %collective-permute-start = (bf16[128,256]{1,0:T(8,128)(2,1)S(1)}, bf16[128,256]{1,0:T(8,128)(2,1)S(1)}, u32[]{:S(2)}, u32[]{:S(2)}) collective-permute-start(bf16[128,256]{1,0:T(8,128)(2,1)S(1)} %get-tuple-element.236), channel_id=1, source_target_pairs={{0,2},{2,4},{4,6},{6,8},{8,10},{10,12},{12,14},{14,0},{1,3},{3,5},... | collective-permute-start | bytes 196616 | tf_op jit(solution)/shard_map/ppermute | solution.py:29
  73.2 12.9 %all-to-all-start.1 = ((f32[8,128,2]{1,2,0:T(2,128)}), f32[8,128,2]{1,2,0:T(2,128)S(1)}, u32[]{:S(2)}, u32[]{:S(2)}) async-start(f32[8,128,2]{1,2,0:T(2,128)} %multiply_bitcast_fusion), calls=%async_computation.1 | async-start | bytes 16384 | tf_op jit(solution)/shard_map/all_to_all | solution.py:170
  77.7 9.7 %collective-permute-start.1 = (bf16[128,256]{1,0:T(8,128)(2,1)S(1)}, bf16[128,256]{1,0:T(8,128)(2,1)S(1)}, u32[]{:S(2)}, u32[]{:S(2)}) collective-permute-start(bf16[128,256]{1,0:T(8,128)(2,1)S(1)} %get-tuple-element.235), channel_id=1, source_target_pairs={{0,4},{2,6},{4,8},{6,10},{8,12},{10,14},{12,0},{14,2},{1,5},{3,7},... | collective-permute-start | bytes 196616 | tf_op jit(solution)/shard_map/ppermute | solution.py:29
  79.8 9.2 %collective-permute-start.2 = (bf16[128,256]{1,0:T(8,128)(2,1)S(1)}, bf16[128,256]{1,0:T(8,128)(2,1)S(1)}, u32[]{:S(2)}, u32[]{:S(2)}) collective-permute-start(bf16[128,256]{1,0:T(8,128)(2,1)S(1)} %get-tuple-element.234), channel_id=1, source_target_pairs={{0,6},{2,8},{4,10},{6,12},{8,14},{10,0},{12,2},{14,4},{1,7},{3,9},... | collective-permute-start | bytes 196616 | tf_op jit(solution)/shard_map/ppermute | solution.py:29
  82.2 7.8 %collective-permute-start.3 = (bf16[128,256]{1,0:T(8,128)(2,1)S(1)}, bf16[128,256]{1,0:T(8,128)(2,1)S(1)}, u32[]{:S(2)}, u32[]{:S(2)}) collective-permute-start(bf16[128,256]{1,0:T(8,128)(2,1)S(1)} %get-tuple-element.233), channel_id=1, source_target_pairs={{0,8},{2,10},{4,12},{6,14},{8,0},{10,2},{12,4},{14,6},{1,9},{3,11}... | collective-permute-start | bytes 196616 | tf_op jit(solution)/shard_map/ppermute | solution.py:29
  83.6 6.3 %collective-permute-start.4 = (bf16[128,256]{1,0:T(8,128)(2,1)S(1)}, bf16[128,256]{1,0:T(8,128)(2,1)S(1)}, u32[]{:S(2)}, u32[]{:S(2)}) collective-permute-start(bf16[128,256]{1,0:T(8,128)(2,1)S(1)} %get-tuple-element.232), channel_id=1, source_target_pairs={{0,10},{2,12},{4,14},{6,0},{8,2},{10,4},{12,6},{14,8},{1,11},{3,13... | collective-permute-start | bytes 196616 | tf_op jit(solution)/shard_map/ppermute | solution.py:29
  86.0 4.7 %collective-permute-start.5 = (bf16[128,256]{1,0:T(8,128)(2,1)S(1)}, bf16[128,256]{1,0:T(8,128)(2,1)S(1)}, u32[]{:S(2)}, u32[]{:S(2)}) collective-permute-start(bf16[128,256]{1,0:T(8,128)(2,1)S(1)} %get-tuple-element.231), channel_id=1, source_target_pairs={{0,12},{2,14},{4,0},{6,2},{8,4},{10,6},{12,8},{14,10},{1,13},{3,15... | collective-permute-start | bytes 196616 | tf_op jit(solution)/shard_map/ppermute | solution.py:29
  87.5 4.3 %collective-permute-start.6 = (bf16[128,256]{1,0:T(8,128)(2,1)S(1)}, bf16[128,256]{1,0:T(8,128)(2,1)S(1)}, u32[]{:S(2)}, u32[]{:S(2)}) collective-permute-start(bf16[128,256]{1,0:T(8,128)(2,1)S(1)} %get-tuple-element.230), channel_id=1, source_target_pairs={{0,14},{2,0},{4,2},{6,4},{8,6},{10,8},{12,10},{14,12},{1,15},{3,1}... | collective-permute-start | bytes 196616 | tf_op jit(solution)/shard_map/ppermute | solution.py:29
